TPU v7x, 256 devices: a whole 4x4x8 slice. The times are simulated.
256 devices in a mesh: dp: 4 (over x_lo, core), expert: 64 (over z, y, x_hi).
Axes of the slice: x: 4 (x_hi: 2, x_lo: 2; x = x_hi * 2 + x_lo), y: 4, z: 8, core: 2. Of those that a mesh axis runs over, the one named last changes fastest.
Arguments:
- prev_acts: bfloat16 [4, 64, 128, 3584], P('dp', 'expert'), may hold values from -6 to 6
- prev_cot: bfloat16 [4, 64, 128, 512], P('dp', 'expert'), may hold values from -0.59765625 to 0.59765625
- weights: bfloat16 [64, 3584, 512], P('expert', 'dp'), may hold values from -0.09375 to 0.09375
- first_moment: float32 [64, 3584, 512], P('expert', 'dp'), may hold values from -1.8 to 1.8
- second_moment: float32 [64, 3584, 512], P('expert', 'dp'), may hold values from 0.1 to 2
- tokens: bfloat16 [4, 64, 128, 3584], P('dp', 'expert'), may hold values from -6 to 6
- routing: int32 [4, 64, 128, 2], P('dp', 'expert'), may hold values from 0 to 15, all different within a row; in each aligned block of 128 rows (0 to 127, 128 to 255, ..., all dimensions but the last counted through in order) at most 24 rows name the same one
- gates: bfloat16 [4, 64, 128, 2], P('dp', 'expert'), may hold values from 0.19921875 to 1
- token_counts: int32 [4, 64], P('dp', 'expert'), may hold values from 64 to 128
- old_owner: int32 [16], replicated, may hold values from 0 to 15, each once
- new_owner: int32 [16], replicated, may hold values from 0 to 15, each once
Outputs:
- expert_hidden: bfloat16 [4, 64, 1536, 256], P('dp', 'expert')
- new_weights: bfloat16 [64, 3584, 512], P('expert', 'dp')
- new_first: float32 [64, 3584, 512], P('expert', 'dp')
- new_second: float32 [64, 3584, 512], P('expert', 'dp')
Inputs may be any that keep to these rules, and one draw needn't show every extreme that they name: `routing`: each token names 2 different hot experts; within the rows of one device no hot expert is named by more than 24 rows. `old_owner`: each is a permutation of the 16 groups. `new_owner`: each is a permutation of the 16 groups.
All inputs are finite; a program needn't handle non-finite values.
Results may differ from a plain program's by a relative error of at most 0.013.
Values may be sent and summed in bfloat16 or wider, within the bound.
No kernel may reach another device: no remote copies, remote signals or barrier semaphores. Data moves between devices by JAX's collectives and lax.ppermute only.
A program may use at most 128 MiB of HBM per device.

v0:
```python
import jax
import jax.numpy as jnp
from jax import lax
from jax.sharding import Mesh
from jax.sharding import PartitionSpec as P

D = 3584
GRP = 4
SCALE_PAD = 128
beta_first = 0.9
beta_second = 0.95
learning = 0.00022
decay_rate = 0.1
epsilon = 1e-08
first_fix = 1.0 - 0.9**40
second_fix = 1.0 - 0.95**40


def adamw(weight_now, first_now, second_now, gradient):
    first_next = beta_first * first_now + (1.0 - beta_first) * gradient
    second_next = beta_second * second_now + (1.0 - beta_second) * gradient * gradient
    stepped = weight_now.astype(jnp.float32) * (1.0 - learning * decay_rate) - learning * (
        first_next / first_fix
    ) / (jnp.sqrt(second_next / second_fix) + epsilon)
    return (stepped.astype(jnp.bfloat16), first_next, second_next)


def migrate(state, group_source, groups, mode=None):
    layers, rows_dev, width = state.shape
    piece_rows = rows_dev // groups
    split = state.reshape(layers, groups, piece_rows, width)
    spread = lax.all_to_all(split, "grp", split_axis=1, concat_axis=1, tiled=True)
    chosen = jnp.take(spread, group_source, axis=1, mode=mode)
    home = lax.all_to_all(chosen, "grp", split_axis=1, concat_axis=1, tiled=True)
    return home.reshape(layers, rows_dev, width)


def pack_tokens(token_block, route_block, gate_block, limit, hot_index, capacity):
    valid = jnp.arange(token_block.shape[0], dtype=jnp.int32) < limit
    hits = (route_block[:, :, None] == hot_index[None, None, :]) & valid[:, None, None]
    named = jnp.sum(hits.astype(jnp.int32), axis=1)
    scales = jnp.sum(jnp.where(hits, gate_block.astype(jnp.float32)[:, :, None], 0.0), axis=1)
    ranks = jnp.cumsum(named, axis=0) - named
    slots = jnp.arange(capacity, dtype=jnp.int32)
    placed = (ranks.T[:, None, :] == slots[None, :, None]) & (named.T[:, None, :] == 1)
    packed = jnp.einsum(
        "hct,td->hcd", placed.astype(jnp.bfloat16), token_block, preferred_element_type=jnp.float32
    ).astype(jnp.bfloat16)
    gate_scale = jnp.einsum("hct,th->hc", placed.astype(jnp.float32), scales).astype(jnp.bfloat16)
    return (packed, gate_scale)


def local(
    prev_acts,
    prev_cot,
    weights,
    first_moment,
    second_moment,
    tokens,
    routing,
    gates,
    token_counts,
    old_owner,
    new_owner,
):
    groups = lax.axis_size("grp")
    experts = groups * GRP
    token_slots = tokens.shape[2]
    capacity = min(token_slots, 3 * token_slots // groups)
    width = weights.shape[2]
    hidden_units = width // 2
    activations = prev_acts[0, 0]
    cotangent = prev_cot[0, 0]
    hot_index = jnp.arange(groups, dtype=jnp.int32)
    holder = jnp.sum(
        jnp.where(new_owner[None, :] == hot_index[:, None], hot_index[None, :], 0), axis=1
    )
    group_source = jnp.take(old_owner, holder)
    packed, gate_scale = pack_tokens(
        tokens[0, 0], routing[0, 0], gates[0, 0], token_counts[0, 0], holder, capacity
    )
    scale_cols = jnp.zeros((groups, capacity, SCALE_PAD), jnp.bfloat16).at[:, :, 0].set(gate_scale)
    payload = jnp.concatenate([packed, scale_cols], axis=2)
    by_group = lax.all_to_all(payload, "grp", split_axis=0, concat_axis=0, tiled=True)
    grads = lax.psum_scatter(
        lax.dot_general(
            activations, cotangent, (((0,), (0,)), ((), ())), preferred_element_type=jnp.float32
        ).astype(jnp.bfloat16),
        "dp",
        scatter_dimension=0,
        tiled=True,
    )
    by_group, grads = lax.optimization_barrier((by_group, grads))
    grads = grads.astype(jnp.float32)
    near = lax.all_gather(by_group, "ylo", axis=0, tiled=False)
    near = near.reshape(2 * groups * capacity, D + SCALE_PAD)
    stepped, first_next, second_next = adamw(weights[0], first_moment[0], second_moment[0], grads)
    weight_home = migrate(stepped[None], group_source, groups)
    new_weight = weight_home[0]
    moments = jnp.stack([first_next.astype(jnp.bfloat16), second_next.astype(jnp.bfloat16)])
    moments, new_weight = lax.optimization_barrier((moments, new_weight))
    moved = migrate(moments, group_source, groups, mode="clip")
    both = lax.all_gather(new_weight, ("xhi", "dp"), axis=0, tiled=True)
    both = both.reshape(2, -1, width)
    both = jnp.pad(both, ((0, 0), (0, SCALE_PAD), (0, 0)))
    projected = jnp.stack(
        [jnp.dot(near, both[k], preferred_element_type=jnp.float32) for k in range(2)]
    )
    scaling = near[:, D].astype(jnp.float32)
    result = (
        jax.nn.silu(projected[:, :, :hidden_units])
        * projected[:, :, hidden_units:]
        * scaling[None, :, None]
    ).astype(jnp.bfloat16)
    xhi = lax.axis_index("xhi")
    own = lax.dynamic_index_in_dim(result, xhi, axis=0, keepdims=False)
    other = lax.dynamic_index_in_dim(result, 1 - xhi, axis=0, keepdims=False)
    for_partner = lax.ppermute(other, "xhi", perm=[(0, 1), (1, 0)])
    mine = jnp.where(
        xhi == 0, jnp.stack([own, for_partner]), jnp.stack([for_partner, own])
    ).reshape(2, 2, groups, capacity, hidden_units)
    hidden = jnp.transpose(mine, (2, 1, 0, 3, 4)).reshape(1, 1, experts * capacity, hidden_units)
    return (
        hidden,
        weight_home,
        moved[0].astype(jnp.float32)[None],
        moved[1].astype(jnp.float32)[None],
    )


def solution(mesh):
    n_dp = mesh.shape["dp"]
    n_expert = mesh.shape["expert"]
    mesh4 = Mesh(mesh.devices.reshape(n_dp, n_expert // GRP, 2, 2), ("dp", "grp", "ylo", "xhi"))
    ex = ("grp", "ylo", "xhi")
    in_specs = (
        P("dp", ex, None, None),
        P("dp", ex, None, None),
        P(ex, "dp", None),
        P(ex, "dp", None),
        P(ex, "dp", None),
        P("dp", ex, None, None),
        P("dp", ex, None, None),
        P("dp", ex, None, None),
        P("dp", ex),
        P(),
        P(),
    )
    out_specs = (P("dp", ex, None, None), P(ex, "dp", None), P(ex, "dp", None), P(ex, "dp", None))
    return jax.shard_map(local, mesh=mesh4, in_specs=in_specs, out_specs=out_specs, check_vma=False)
```

profile of v0, /device:TPU:6, one launch (start us, length us, event | category | flops | bytes accessed | tf_op | source)
XLA Modules:
  0.0 284.6 jit_solution(10818399610023016619)
XLA Ops:
  7.2 1.1 copy-done
  8.3 3.8 %convolution_convert_fusion = bf16[3584,512]{1,0:T(8,128)(2,1)} fusion(bf16[1,1,128,3584]{3,2,1,0:T(8,128)(2,1)S(1)} %copy-done, bf16[1,1,128,512]{3,2,1,0:T(8,128)(2,1)} %param.14), kind=kOutput, calls=%fused_computation.5 | convolution fusion | flops 471597056 | bytes 4718592 | tf_op jit(solution)/shard_map/dot_general | solution.py:86
  14.5 0.9 convolution_convert_fusion.1
  15.6 80.3 %all_to_all.25 = bf16[16,24,3712]{2,1,0:T(8,128)(2,1)} all-to-all(bf16[16,24,3712]{2,1,0:T(8,128)(2,1)S(1)} %fusion.7), channel_id=1, replica_groups=mesh['dp'=4,'grp'=16,'ylo'=2,'xhi'=2] {'grp'}, dimensions={0} | all-to-all | bytes 5701632 | tf_op jit(solution)/shard_map/all_to_all | solution.py:84
  96.0 1.1 copy-done.5
  97.1 5.1 %fusion.10 = (bf16[896,512]{1,0:T(8,128)(2,1)}, bf16[1,896,512]{2,1,0:T(8,128)(2,1)S(1)}, bf16[1,896,512]{2,1,0:T(8,128)(2,1)}) fusion(bf16[1,896,512]{2,1,0:T(8,128)(2,1)S(1)} %copy-done.5, bf16[896,512]{1,0:T(8,128)(2,1)} %reduce-scatter.2.cloned.1.call-done, f32[1,896,512]{2,1,0:T(8,128)} %param.16, f32[1,896,512]{2,1,0:T(8,128)} %param.17), kind=kLoop, calls=%fused_computation.22 | loop fusion | flops 8257536 | bytes 8257536 | tf_op jit(solution)/shard_map/convert_element_type | solution.py:25
  102.3 3.8 %all-to-all-start.1 = ((bf16[1,16,56,512]{3,2,0,1:T(8,128)(2,1)}), bf16[1,16,56,512]{3,2,0,1:T(8,128)(2,1)S(1)}, u32[]{:S(2)}, u32[]{:S(2)}) async-start(bf16[1,16,56,512]{3,2,0,1:T(8,128)(2,1)} %bitcast.125), calls=%async_computation.2 | async-start | bytes 1835008 | tf_op jit(solution)/shard_map/all_to_all | solution.py:32
  106.1 0.7 gather_fusion
  106.8 24.6 %all-to-all-done.1 = bf16[1,16,56,512]{3,2,0,1:T(8,128)(2,1)S(1)} async-done(((bf16[1,16,56,512]{3,2,0,1:T(8,128)(2,1)}), bf16[1,16,56,512]{3,2,0,1:T(8,128)(2,1)S(1)}, u32[]{:S(2)}, u32[]{:S(2)}) %all-to-all-start.1) | async-done | bytes 917536 | tf_op jit(solution)/shard_map/all_to_all | solution.py:32
  131.4 1.5 gather_fusion.1
  132.9 2.2 fusion.26
  135.2 3.8 %all-to-all-start.2 = ((bf16[1,16,56,512]{3,2,0,1:T(8,128)(2,1)}), bf16[1,16,56,512]{3,2,0,1:T(8,128)(2,1)S(1)}, u32[]{:S(2)}, u32[]{:S(2)}) async-start(bf16[1,16,56,512]{3,2,0,1:T(8,128)(2,1)} %fusion.26), calls=%async_computation.3 | async-start | bytes 1835008 | tf_op jit(solution)/shard_map/all_to_all | solution.py:34
  139.0 2.6 pad_maximum_fusion
  141.6 24.7 %all-to-all-done.2 = bf16[1,16,56,512]{3,2,0,1:T(8,128)(2,1)S(1)} async-done(((bf16[1,16,56,512]{3,2,0,1:T(8,128)(2,1)}), bf16[1,16,56,512]{3,2,0,1:T(8,128)(2,1)S(1)}, u32[]{:S(2)}, u32[]{:S(2)}) %all-to-all-start.2) | async-done | bytes 917536 | tf_op jit(solution)/shard_map/all_to_all | solution.py:34
  166.4 0.9 copy-done.2
  167.3 3.0 %copy.50 = bf16[2,16,56,512]{3,2,0,1:T(8,128)(2,1)} copy(bf16[2,16,56,512]{3,2,1,0:T(8,128)(2,1)} %bitcast.120) | data formatting | bytes 3670016 | tf_op jit(solution)/shard_map/reshape | solution.py:31
  170.3 3.7 %all-to-all-start.3 = ((bf16[2,16,56,512]{3,2,0,1:T(8,128)(2,1)}), bf16[2,16,56,512]{3,2,0,1:T(8,128)(2,1)S(1)}, u32[]{:S(2)}, u32[]{:S(2)}) async-start(bf16[2,16,56,512]{3,2,0,1:T(8,128)(2,1)} %copy.50), calls=%async_computation.4 | async-start | bytes 3670016 | tf_op jit(solution)/shard_map/all_to_all | solution.py:32
  174.0 45.9 %all-to-all-done.3 = bf16[2,16,56,512]{3,2,0,1:T(8,128)(2,1)S(1)} async-done(((bf16[2,16,56,512]{3,2,0,1:T(8,128)(2,1)}), bf16[2,16,56,512]{3,2,0,1:T(8,128)(2,1)S(1)}, u32[]{:S(2)}, u32[]{:S(2)}) %all-to-all-start.3) | async-done | bytes 1835040 | tf_op jit(solution)/shard_map/all_to_all | solution.py:32
  219.9 1.9 gather_fusion.2
  221.7 3.7 %all-to-all-start.4 = ((bf16[2,16,56,512]{3,2,0,1:T(8,128)(2,1)}), bf16[2,16,56,512]{3,2,0,1:T(8,128)(2,1)S(1)}, u32[]{:S(2)}, u32[]{:S(2)}) async-start(bf16[2,16,56,512]{3,2,0,1:T(8,128)(2,1)} %bitcast.121), calls=%async_computation.5 | async-start | bytes 3670016 | tf_op jit(solution)/shard_map/all_to_all | solution.py:34
  225.5 0.9 slice.57
  226.6 14.0 %all-gather.4.cloned.1.call-done = bf16[7168,512]{1,0:T(8,128)(2,1)} async-done(((bf16[896,512]{1,0:T(8,128)(2,1)}), bf16[7168,512]{1,0:T(8,128)(2,1)}) %all-gather.4.cloned.1.call-update) | async-done | bytes 7340048 | tf_op jit(solution)/shard_map/all_gather | solution.py:103
  240.6 6.3 %fusion.15 = f32[1,768,512]{2,1,0:T(8,128)S(1)} fusion(bf16[768,3712]{1,0:T(8,128)(2,1)} %bitcast.131, bf16[2,3584,512]{2,1,0:T(8,128)(2,1)} %bitcast.135), kind=kOutput, calls=%fused_computation.28 | convolution fusion | flops 2919235584 | bytes 14614528 | tf_op jit(solution)/shard_map/dot_general | solution.py:107
  247.0 1.2 copy-done.8
  248.1 3.1 %fusion.18 = f32[1,768,512]{2,1,0:T(8,128)S(1)} fusion(bf16[768,3712]{1,0:T(8,128)(2,1)S(1)} %bitcast.132, bf16[2,3584,512]{2,1,0:T(8,128)(2,1)S(1)} %bitcast.136), kind=kOutput, calls=%fused_computation.29 | convolution fusion | flops 2919235584 | bytes 14614528 | tf_op jit(solution)/shard_map/dot_general | solution.py:107
  251.7 2.5 collective-permute-start
  254.3 17.5 %all-to-all-done.4 = bf16[2,16,56,512]{3,2,0,1:T(8,128)(2,1)S(1)} async-done(((bf16[2,16,56,512]{3,2,0,1:T(8,128)(2,1)}), bf16[2,16,56,512]{3,2,0,1:T(8,128)(2,1)S(1)}, u32[]{:S(2)}, u32[]{:S(2)}) %all-to-all-start.4) | async-done | bytes 1835040 | tf_op jit(solution)/shard_map/all_to_all | solution.py:34
  271.9 1.5 convert.5
  273.4 1.5 convert.6
  274.9 1.3 fusion.28
  276.2 1.0 copy.49
  277.1 0.9 copy.56
  (52 shorter events, 2.8 us)
Async XLA Ops:
  7.2 1.2 copy-start
  7.2 88.7 %reduce-scatter.2.cloned.1.call-start = ((), (), s32[]{:S(2)}) async-start(), calls=%async_computation.6 | async-start | bytes 4587520 | tf_op jit(solution)/shard_map/reduce_scatter | solution.py:85
  12.2 0.7 copy-start.9
  12.2 1.4 copy-start.7
  12.2 1.9 copy-start.10
  12.2 2.3 copy-start.4
  12.2 213.3 %all-gather.6.cloned.1.call-start = ((), (), s32[]{:S(2)}) async-start(), calls=%async_computation.8 | async-start | bytes 8552448 | tf_op jit(solution)/shard_map/all_gather | solution.py:95
  95.9 1.2 copy-start.5
  102.2 3.8 %copy-start.1 = (s32[16]{0:T(128)S(1)}, s32[16]{0:T(128)}, u32[]{:S(2)}) copy-start(s32[16]{0:T(128)} %param.22) | copy-start | bytes 196
  102.3 29.1 %all-to-all-start.1 = ((bf16[1,16,56,512]{3,2,0,1:T(8,128)(2,1)}), bf16[1,16,56,512]{3,2,0,1:T(8,128)(2,1)S(1)}, u32[]{:S(2)}, u32[]{:S(2)}) async-start(bf16[1,16,56,512]{3,2,0,1:T(8,128)(2,1)} %bitcast.125), calls=%async_computation.2 | async-start | bytes 1835008 | tf_op jit(solution)/shard_map/all_to_all | solution.py:32
  135.2 31.2 %all-to-all-start.2 = ((bf16[1,16,56,512]{3,2,0,1:T(8,128)(2,1)}), bf16[1,16,56,512]{3,2,0,1:T(8,128)(2,1)S(1)}, u32[]{:S(2)}, u32[]{:S(2)}) async-start(bf16[1,16,56,512]{3,2,0,1:T(8,128)(2,1)} %fusion.26), calls=%async_computation.3 | async-start | bytes 1835008 | tf_op jit(solution)/shard_map/all_to_all | solution.py:34
  139.0 101.6 %all-gather.4.cloned.1.call-start = ((), (), s32[]{:S(2)}) async-start(), calls=%async_computation.7 | async-start | bytes 8257536 | tf_op jit(solution)/shard_map/all_gather | solution.py:103
  166.4 0.9 copy-start.2
  170.3 49.6 %all-to-all-start.3 = ((bf16[2,16,56,512]{3,2,0,1:T(8,128)(2,1)}), bf16[2,16,56,512]{3,2,0,1:T(8,128)(2,1)S(1)}, u32[]{:S(2)}, u32[]{:S(2)}) async-start(bf16[2,16,56,512]{3,2,0,1:T(8,128)(2,1)} %copy.50), calls=%async_computation.4 | async-start | bytes 3670016 | tf_op jit(solution)/shard_map/all_to_all | solution.py:32
  221.7 50.0 %all-to-all-start.4 = ((bf16[2,16,56,512]{3,2,0,1:T(8,128)(2,1)}), bf16[2,16,56,512]{3,2,0,1:T(8,128)(2,1)S(1)}, u32[]{:S(2)}, u32[]{:S(2)}) async-start(bf16[2,16,56,512]{3,2,0,1:T(8,128)(2,1)} %bitcast.121), calls=%async_computation.5 | async-start | bytes 3670016 | tf_op jit(solution)/shard_map/all_to_all | solution.py:34
  240.6 6.3 %copy-start.6 = (bf16[32,24,3712]{2,1,0:T(8,128)(2,1)S(1)}, bf16[32,24,3712]{2,1,0:T(8,128)(2,1)}, u32[]{:S(2)}) copy-start(bf16[32,24,3712]{2,1,0:T(8,128)(2,1)} %all-gather.6.cloned.1.call-done) | copy-start | bytes 17104900
  240.6 7.5 %copy-start.8 = (bf16[7168,512]{1,0:T(8,128)(2,1)S(1)}, bf16[7168,512]{1,0:T(8,128)(2,1)}, u32[]{:S(2)}) copy-start(bf16[7168,512]{1,0:T(8,128)(2,1)} %all-gather.4.cloned.1.call-done) | copy-start | bytes 22020100
  251.7 23.1 %collective-permute-start = (bf16[768,256]{1,0:T(8,128)(2,1)S(1)}, bf16[768,256]{1,0:T(8,128)(2,1)}, u32[]{:S(2)}, u32[]{:S(2)}) collective-permute-start(bf16[768,256]{1,0:T(8,128)(2,1)S(1)} %get-tuple-element.30), channel_id=1, source_target_pairs={{0,1},{1,0},{2,3},{3,2},{4,5},{5,4},{6,7},{7,6},{8,9},{9,8},{10,11... | collective-permute-start | bytes 1179656 | tf_op jit(solution)/shard_map/ppermute | solution.py:118
  274.8 2.3 copy-start.3
Sparse Core Ops, SparseCore 0:
  12.3 45.8 reduce-scatter.1
  96.1 95.5 all-gather.5
  194.1 46.5 all-gather.3
where the time goes:
time: 285 us
  waiting for transfers between devices  127 us (45%)
  blocking collectives  80.3 us (28%)
  starting transfers between devices  17.7 us (6%)
  local copies, waits for them, and re-layouts  15.5 us (5%)
  other arithmetic  15.4 us (5%)
  between operations  14.6 us (5%)
  matrix products  14.2 us (5%)
    all_to_all x1, blocking collectives, local(): lax.all_to_all(payload, 'grp', split_axis=0, concat_axis=0, tiled=True)  80.3 us
    all_to_all x2, waiting for transfers between devices, migrate(): lax.all_to_all(split, 'grp', split_axis=1, concat_axis=1, tiled=True)  70.5 us
    all_to_all x2, waiting for transfers between devices, migrate(): lax.all_to_all(chosen, 'grp', split_axis=1, concat_axis=1, tiled=True)  42.2 us
    all_gather x1, waiting for transfers between devices, local(): both = lax.all_gather(new_weight, ('xhi', 'dp'), axis=0, tiled=True)  14 us
    dot_general x2, matrix products, local(): jnp.dot(near, both[k], preferred_element_type=jnp.float32)  9.38 us
    all_to_all x2, starting transfers between devices, migrate(): lax.all_to_all(chosen, 'grp', split_axis=1, concat_axis=1, tiled=True)  7.54 us
    all_to_all x2, starting transfers between devices, migrate(): lax.all_to_all(split, 'grp', split_axis=1, concat_axis=1, tiled=True)  7.49 us
    unnamed x24, local copies, waits for them, and re-layouts  6 us
  transfers between devices with their start and end apart: 8, of which 5 were waited for; matrix products, arithmetic and copies ran while one was open for 12% of the time, Pallas kernels for 0%

commit v1 on v0

--- a/solution.py
+++ b/solution.py
@@ -16,6 +16,12 @@
 second_fix = 1.0 - 0.95**40
 
 
+def swap_blocks(value, mesh_axis, split, join):
+    pieces = jnp.split(value, lax.axis_size(mesh_axis), axis=split)
+    incoming = lax.all_to_all(jnp.stack(pieces), mesh_axis, 0, 0)
+    return jnp.concatenate(incoming, axis=join)
+
+
 def adamw(weight_now, first_now, second_now, gradient):
     first_next = beta_first * first_now + (1.0 - beta_first) * gradient
     second_next = beta_second * second_now + (1.0 - beta_second) * gradient * gradient
@@ -31,7 +37,7 @@
     split = state.reshape(layers, groups, piece_rows, width)
     spread = lax.all_to_all(split, "grp", split_axis=1, concat_axis=1, tiled=True)
     chosen = jnp.take(spread, group_source, axis=1, mode=mode)
-    home = lax.all_to_all(chosen, "grp", split_axis=1, concat_axis=1, tiled=True)
+    home = swap_blocks(chosen, "grp", 1, 1)
     return home.reshape(layers, rows_dev, width)
 
 

time: 285 us -> 311 us (1.091)
  local copies, waits for them, and re-layouts: 15.5 us -> 42.2 us
    unnamed x24 -> x56, local copies, waits for them, and re-layouts: 6 us -> 31.4 us
    all_to_all x2, waiting for transfers between devices: 42.2 us -> 57 us  [swap_blocks(): incoming = lax.all_to_all(jnp.stack(pieces), mesh_axis, 0, 0)]
    all_gather x1, waiting for transfers between devices: 14 us -> 0.02 us  [local(): both = lax.all_gather(new_weight, ('xhi', 'dp'), axis=0, tiled=True)]
  transfers between devices with their start and end apart: 8 -> 8, of which waited for: 5 -> 4; matrix products, arithmetic and copies ran while one was open for 12% -> 18% of each run, Pallas kernels for 0% -> 0%
where the time goes in v1:
time: 311 us; the launch traced here: 310 us
  waiting for transfers between devices  128 us (41%)
  blocking collectives  80.4 us (26%)
  local copies, waits for them, and re-layouts  42.2 us (14%)
  starting transfers between devices  16.7 us (5%)
  between operations  14.7 us (5%)
  other arithmetic  14.5 us (5%)
  matrix products  14.2 us (5%)
    all_to_all x1, blocking collectives, local(): lax.all_to_all(payload, 'grp', split_axis=0, concat_axis=0, tiled=True)  80.4 us
    all_to_all x2, waiting for transfers between devices, migrate(): lax.all_to_all(split, 'grp', split_axis=1, concat_axis=1, tiled=True)  70.6 us
    all_to_all x2, waiting for transfers between devices, swap_blocks(): incoming = lax.all_to_all(jnp.stack(pieces), mesh_axis, 0, 0)  57 us
    unnamed x56, local copies, waits for them, and re-layouts  31.4 us
    dot_general x2, matrix products, local(): jnp.dot(near, both[k], preferred_element_type=jnp.float32)  9.39 us
    all_to_all x2, starting transfers between devices, swap_blocks(): incoming = lax.all_to_all(jnp.stack(pieces), mesh_axis, 0, 0)  7.59 us
    all_to_all x2, starting transfers between devices, migrate(): lax.all_to_all(split, 'grp', split_axis=1, concat_axis=1, tiled=True)  7.48 us
  transfers between devices with their start and end apart: 8, of which 4 were waited for; matrix products, arithmetic and copies ran while one was open for 18% of the time, Pallas kernels for 0%

profile of v1, /device:TPU:6, one launch (start us, length us, event | category | flops | bytes accessed | tf_op | source)
XLA Modules:
  0.0 310.5 jit_solution(4107325109135792310)
XLA Ops:
  7.2 1.1 copy-done
  8.3 3.8 %convolution_convert_fusion = bf16[3584,512]{1,0:T(8,128)(2,1)} fusion(bf16[1,1,128,3584]{3,2,1,0:T(8,128)(2,1)S(1)} %copy-done, bf16[1,1,128,512]{3,2,1,0:T(8,128)(2,1)} %param.14), kind=kOutput, calls=%fused_computation.5 | convolution fusion | flops 471597056 | bytes 4718592 | tf_op jit(solution)/shard_map/dot_general | solution.py:92
  15.6 80.4 %all_to_all.25 = bf16[16,24,3712]{2,1,0:T(8,128)(2,1)} all-to-all(bf16[16,24,3712]{2,1,0:T(8,128)(2,1)S(1)} %fusion.7), channel_id=1, replica_groups=mesh['dp'=4,'grp'=16,'ylo'=2,'xhi'=2] {'grp'}, dimensions={0} | all-to-all | bytes 5701632 | tf_op jit(solution)/shard_map/all_to_all | solution.py:90
  96.1 5.1 %fusion.10 = (bf16[896,512]{1,0:T(8,128)(2,1)}, bf16[1,896,512]{2,1,0:T(8,128)(2,1)S(1)}, bf16[1,896,512]{2,1,0:T(8,128)(2,1)}) fusion(bf16[1,896,512]{2,1,0:T(8,128)(2,1)S(1)} %copy-done.6, bf16[896,512]{1,0:T(8,128)(2,1)} %reduce-scatter.2.cloned.1.call-done, f32[1,896,512]{2,1,0:T(8,128)} %param.16, f32[1,896,512]{2,1,0:T(8,128)} %param.17), kind=kLoop, calls=%fused_computation.22 | loop fusion | flops 8257536 | bytes 8257536 | tf_op jit(solution)/shard_map/convert_element_type | solution.py:31
  101.2 3.8 %all-to-all-start.1 = ((bf16[1,16,56,512]{3,2,0,1:T(8,128)(2,1)}), bf16[1,16,56,512]{3,2,0,1:T(8,128)(2,1)S(1)}, u32[]{:S(2)}, u32[]{:S(2)}) async-start(bf16[1,16,56,512]{3,2,0,1:T(8,128)(2,1)} %bitcast.266), calls=%async_computation.2 | async-start | bytes 1835008 | tf_op jit(solution)/shard_map/all_to_all | solution.py:38
  105.8 24.6 %all-to-all-done.1 = bf16[1,16,56,512]{3,2,0,1:T(8,128)(2,1)S(1)} async-done(((bf16[1,16,56,512]{3,2,0,1:T(8,128)(2,1)}), bf16[1,16,56,512]{3,2,0,1:T(8,128)(2,1)S(1)}, u32[]{:S(2)}, u32[]{:S(2)}) %all-to-all-start.1) | async-done | bytes 917536 | tf_op jit(solution)/shard_map/all_to_all | solution.py:38
  130.4 1.5 gather_fusion.1
  131.9 1.3 bitcast_select_fusion
  143.3 3.9 %all-to-all-start.2 = ((bf16[16,1,1,56,512]{4,3,2,1,0:T(8,128)(2,1)}), bf16[16,1,1,56,512]{4,3,2,1,0:T(8,128)(2,1)S(1)}, u32[]{:S(2)}, u32[]{:S(2)}) async-start(bf16[16,1,1,56,512]{4,3,2,1,0:T(8,128)(2,1)} %constant_dynamic-update-slice_fusion), calls=%async_computation.3 | async-start | bytes 1835008 | tf_op jit(solution)/shard_map/all_to_all | solution.py:21
  147.2 2.6 pad_maximum_fusion
  149.8 24.5 %all-to-all-done.2 = bf16[16,1,1,56,512]{4,3,2,1,0:T(8,128)(2,1)S(1)} async-done(((bf16[16,1,1,56,512]{4,3,2,1,0:T(8,128)(2,1)}), bf16[16,1,1,56,512]{4,3,2,1,0:T(8,128)(2,1)S(1)}, u32[]{:S(2)}, u32[]{:S(2)}) %all-to-all-start.2) | async-done | bytes 917536 | tf_op jit(solution)/shard_map/all_to_all | solution.py:21
  175.2 3.0 copy.48
  178.2 3.7 %all-to-all-start.3 = ((bf16[2,16,56,512]{3,2,0,1:T(8,128)(2,1)}), bf16[2,16,56,512]{3,2,0,1:T(8,128)(2,1)S(1)}, u32[]{:S(2)}, u32[]{:S(2)}) async-start(bf16[2,16,56,512]{3,2,0,1:T(8,128)(2,1)} %copy.48), calls=%async_computation.4 | async-start | bytes 3670016 | tf_op jit(solution)/shard_map/all_to_all | solution.py:38
  181.9 46.0 %all-to-all-done.3 = bf16[2,16,56,512]{3,2,0,1:T(8,128)(2,1)S(1)} async-done(((bf16[2,16,56,512]{3,2,0,1:T(8,128)(2,1)}), bf16[2,16,56,512]{3,2,0,1:T(8,128)(2,1)S(1)}, u32[]{:S(2)}, u32[]{:S(2)}) %all-to-all-start.3) | async-done | bytes 1835040 | tf_op jit(solution)/shard_map/all_to_all | solution.py:38
  227.9 1.9 gather_fusion.2
  229.8 1.7 fusion.48
  231.5 1.6 fusion.47
  233.1 1.6 fusion.46
  234.6 1.6 fusion.45
  236.2 1.6 fusion.44
  237.7 1.6 fusion.43
  239.3 1.6 fusion.42
  240.8 1.6 fusion.41
  247.6 3.7 %all-to-all-start.4 = ((bf16[16,2,1,56,512]{4,3,1,2,0:T(8,128)(2,1)}), bf16[16,2,1,56,512]{4,3,1,2,0:T(8,128)(2,1)S(1)}, u32[]{:S(2)}, u32[]{:S(2)}) async-start(bf16[16,2,1,56,512]{4,3,1,2,0:T(8,128)(2,1)} %fusion.33), calls=%async_computation.5 | async-start | bytes 3670016 | tf_op jit(solution)/shard_map/all_to_all | solution.py:21
  252.5 6.3 %fusion.15 = f32[1,768,512]{2,1,0:T(8,128)S(1)} fusion(bf16[768,3712]{1,0:T(8,128)(2,1)} %bitcast.272, bf16[2,3584,512]{2,1,0:T(8,128)(2,1)} %bitcast.276), kind=kOutput, calls=%fused_computation.28 | convolution fusion | flops 2919235584 | bytes 14614528 | tf_op jit(solution)/shard_map/dot_general | solution.py:113
  258.9 1.1 copy-done.9
  260.0 3.1 fusion.18
  263.6 1.5 collective-permute-start
  265.1 32.5 %all-to-all-done.4 = bf16[16,2,1,56,512]{4,3,1,2,0:T(8,128)(2,1)S(1)} async-done(((bf16[16,2,1,56,512]{4,3,1,2,0:T(8,128)(2,1)}), bf16[16,2,1,56,512]{4,3,1,2,0:T(8,128)(2,1)S(1)}, u32[]{:S(2)}, u32[]{:S(2)}) %all-to-all-start.4) | async-done | bytes 1835040 | tf_op jit(solution)/shard_map/all_to_all | solution.py:21
  297.8 1.5 convert.5
  299.3 1.5 convert.6
  300.7 1.3 fusion.27
  (86 shorter events, 23.4 us)
Async XLA Ops:
  7.2 1.2 copy-start
  7.2 88.9 %reduce-scatter.2.cloned.1.call-start = ((), (), s32[]{:S(2)}) async-start(), calls=%async_computation.6 | async-start | bytes 4587520 | tf_op jit(solution)/shard_map/reduce_scatter | solution.py:91
  12.2 0.7 copy-start.10
  12.2 1.4 copy-start.8
  12.2 1.9 copy-start.11
  12.2 2.3 copy-start.5
  15.6 80.5 %copy-start.6 = (bf16[1,896,512]{2,1,0:T(8,128)(2,1)S(1)}, bf16[1,896,512]{2,1,0:T(8,128)(2,1)}, u32[]{:S(2)}) copy-start(bf16[1,896,512]{2,1,0:T(8,128)(2,1)} %param.15) | copy-start | bytes 2752516
  101.2 3.9 %copy-start.1 = (s32[16]{0:T(128)S(1)}, s32[16]{0:T(128)}, u32[]{:S(2)}) copy-start(s32[16]{0:T(128)} %param.22) | copy-start | bytes 196
  101.2 29.1 %all-to-all-start.1 = ((bf16[1,16,56,512]{3,2,0,1:T(8,128)(2,1)}), bf16[1,16,56,512]{3,2,0,1:T(8,128)(2,1)S(1)}, u32[]{:S(2)}, u32[]{:S(2)}) async-start(bf16[1,16,56,512]{3,2,0,1:T(8,128)(2,1)} %bitcast.266), calls=%async_computation.2 | async-start | bytes 1835008 | tf_op jit(solution)/shard_map/all_to_all | solution.py:38
  105.0 146.4 %all-gather.6.cloned.1.call-start = ((), (), s32[]{:S(2)}) async-start(), calls=%async_computation.8 | async-start | bytes 8552448 | tf_op jit(solution)/shard_map/all_gather | solution.py:101
  143.3 31.0 %all-to-all-start.2 = ((bf16[16,1,1,56,512]{4,3,2,1,0:T(8,128)(2,1)}), bf16[16,1,1,56,512]{4,3,2,1,0:T(8,128)(2,1)S(1)}, u32[]{:S(2)}, u32[]{:S(2)}) async-start(bf16[16,1,1,56,512]{4,3,2,1,0:T(8,128)(2,1)} %constant_dynamic-update-slice_fusion), calls=%async_computation.3 | async-start | bytes 1835008 | tf_op jit(solution)/shard_map/all_to_all | solution.py:21
  147.1 105.4 %all-gather.4.cloned.1.call-start = ((), (), s32[]{:S(2)}) async-start(), calls=%async_computation.7 | async-start | bytes 8257536 | tf_op jit(solution)/shard_map/all_gather | solution.py:109
  174.3 0.9 copy-start.2
  178.2 49.8 %all-to-all-start.3 = ((bf16[2,16,56,512]{3,2,0,1:T(8,128)(2,1)}), bf16[2,16,56,512]{3,2,0,1:T(8,128)(2,1)S(1)}, u32[]{:S(2)}, u32[]{:S(2)}) async-start(bf16[2,16,56,512]{3,2,0,1:T(8,128)(2,1)} %copy.48), calls=%async_computation.4 | async-start | bytes 3670016 | tf_op jit(solution)/shard_map/all_to_all | solution.py:38
  229.8 12.6 %copy-start.4 = (bf16[16,2,56,512]{3,2,1,0:T(8,128)(2,1)S(1)}, bf16[16,2,56,512]{3,2,1,0:T(8,128)(2,1)}, u32[]{:S(2)}) copy-start(bf16[16,2,56,512]{3,2,1,0:T(8,128)(2,1)} %gather_fusion.2) | copy-start | bytes 5505028
  247.6 50.0 %all-to-all-start.4 = ((bf16[16,2,1,56,512]{4,3,1,2,0:T(8,128)(2,1)}), bf16[16,2,1,56,512]{4,3,1,2,0:T(8,128)(2,1)S(1)}, u32[]{:S(2)}, u32[]{:S(2)}) async-start(bf16[16,2,1,56,512]{4,3,1,2,0:T(8,128)(2,1)} %fusion.33), calls=%async_computation.5 | async-start | bytes 3670016 | tf_op jit(solution)/shard_map/all_to_all | solution.py:21
  252.5 6.3 %copy-start.7 = (bf16[32,24,3712]{2,1,0:T(8,128)(2,1)S(1)}, bf16[32,24,3712]{2,1,0:T(8,128)(2,1)}, u32[]{:S(2)}) copy-start(bf16[32,24,3712]{2,1,0:T(8,128)(2,1)} %all-gather.6.cloned.1.call-done) | copy-start | bytes 17104900
  252.5 7.5 %copy-start.9 = (bf16[7168,512]{1,0:T(8,128)(2,1)S(1)}, bf16[7168,512]{1,0:T(8,128)(2,1)}, u32[]{:S(2)}) copy-start(bf16[7168,512]{1,0:T(8,128)(2,1)} %all-gather.4.cloned.1.call-done) | copy-start | bytes 22020100
  263.6 37.1 %collective-permute-start = (bf16[768,256]{1,0:T(8,128)(2,1)S(1)}, bf16[768,256]{1,0:T(8,128)(2,1)}, u32[]{:S(2)}, u32[]{:S(2)}) collective-permute-start(bf16[768,256]{1,0:T(8,128)(2,1)S(1)} %get-tuple-element.30), channel_id=1, source_target_pairs={{0,1},{1,0},{2,3},{3,2},{4,5},{5,4},{6,7},{7,6},{8,9},{9,8},{10,11... | collective-permute-start | bytes 1179656 | tf_op jit(solution)/shard_map/ppermute | solution.py:124
  300.7 2.3 copy-start.3
Sparse Core Ops, SparseCore 0:
  12.3 45.8 reduce-scatter.1
  107.6 94.5 all-gather.5
  204.6 46.3 all-gather.3
